TPU v7x, 512 devices: a whole 4x8x8 slice. The times are simulated.
512 devices in a mesh: ctx: 64 (over y_lo, z, core), tp: 8 (over y_hi, x).
Axes of the slice: x: 4, y: 8 (y_hi: 2, y_lo: 4; y = y_hi * 4 + y_lo), z: 8, core: 2. Of those that a mesh axis runs over, the one named last changes fastest.
Arguments:
- tokens: bfloat16 [16384, 2048], P('ctx', 'tp'), may hold values from -6 to 6
- w_in: bfloat16 [2048, 4096], P('ctx', 'tp'), may hold values from -0.125 to 0.125
- w_bc: bfloat16 [2048, 2048], P('ctx', 'tp'), may hold values from -0.01171875 to 0.01171875
- w_dt: bfloat16 [2048, 64], P('ctx', 'tp'), may hold values from -0.125 to 0.125
- dt_bias: float32 [64], P('tp'), may hold values from -2 to 0
- decay_rate: float32 [64], P('tp'), may hold values from 1e-05 to 0.1
- skip_gain: float32 [64], P('tp'), may hold values from 0.5 to 1.5
- w_out: bfloat16 [4096, 2048], P('tp', 'ctx'), may hold values from -0.09375 to 0.09375
- cotangent: bfloat16 [16384, 2048], P('ctx', 'tp'), may hold values from -6 to 6
Outputs:
- output: bfloat16 [16384, 2048], P('ctx', 'tp')
- grad: bfloat16 [16384, 2048], P('ctx', 'tp')
All inputs are finite; a program needn't handle non-finite values.
Results may differ from a plain program's by a relative error of at most 0.0061.
Values may be sent and summed in bfloat16 or wider, within the bound.
No kernel may reach another device: no remote copies, remote signals or barrier semaphores. Data moves between devices by JAX's collectives and lax.ppermute only.
A program may use at most 128 MiB of HBM per device.

v0:
```python
import jax
import jax.numpy as jnp
from jax import lax
from jax.sharding import PartitionSpec as P

HEADDIM = 64
STATE = 128
SPAN = 256
HIGH = lax.Precision.HIGH
RING = 4


def both_carries(decay, forward, backward, axis):
    devices, position = (lax.axis_size(axis), lax.axis_index(axis))
    heads = decay.shape[0]
    own_a = decay[:, None]
    own_s = forward.reshape(heads, -1)
    own_u = backward.reshape(heads, -1)
    size = own_s.shape[1]
    message = jnp.concatenate([own_s, own_u, jnp.broadcast_to(own_a, (heads, 128))], axis=1)
    got = lax.ppermute(message, axis, [(i, i ^ 1) for i in range(devices)])
    sib_s = got[:, :size]
    sib_u = got[:, size : 2 * size]
    sib_a = got[:, 2 * size : 2 * size + 1]
    second = position & 1 != 0
    first_a = jnp.where(second, sib_a, own_a)
    first_s = jnp.where(second, sib_s, own_s)
    last_a = jnp.where(second, own_a, sib_a)
    last_s = jnp.where(second, own_s, sib_s)
    first_u = jnp.where(second, sib_u, own_u)
    last_u = jnp.where(second, own_u, sib_u)
    total_a = first_a * last_a
    total_m = jnp.where(second, first_u + first_a * last_u, last_a * first_s + last_s)
    before_a = jnp.ones_like(total_a)
    before_m = jnp.zeros_like(total_m)
    bit = 2
    while bit < devices:
        if 2 * bit >= devices:
            wanted = [(i, i ^ bit) for i in range(devices) if (i & bit != 0) == (i & 1 != 0)]
            got_m = lax.ppermute(total_m, axis, wanted)
            flag = (position & bit != 0) != second
            before_m = jnp.where(flag, before_a * got_m + before_m, before_m)
            break
        message = jnp.concatenate([total_m, jnp.broadcast_to(total_a, (heads, 128))], axis=1)
        got = lax.ppermute(message, axis, [(i, i ^ bit) for i in range(devices)])
        got_m = got[:, :size]
        got_a = got[:, size : size + 1]
        flag = (position & bit != 0) != second
        before_m = jnp.where(flag, before_a * got_m + before_m, before_m)
        before_a = jnp.where(flag, before_a * got_a, before_a)
        total_m = jnp.where(flag, total_a * got_m + total_m, got_a * total_m + got_m)
        total_a = total_a * got_a
        bit *= 2
    got = lax.ppermute(before_m, axis, [(i, i ^ 1) for i in range(devices)])
    state_in = jnp.where(second, first_a * got + first_s, before_m)
    adjoint = jnp.where(second, before_m, last_u + last_a * got)
    return (state_in.reshape(forward.shape), adjoint.reshape(backward.shape))


def scattered_sum(partial, rows_axis, axis, width):
    chains, devices = (lax.axis_size(rows_axis), lax.axis_size(axis))
    chain, position = (lax.axis_index(rows_axis), lax.axis_index(axis))
    ring = RING if devices % RING == 0 else 1

    def label(t, turn):
        return t - t % ring + (t + turn) % ring

    def place(lab, turn):
        return lab - lab % ring + (lab - turn) % ring

    turn = chain % 2
    mine_label = label(position, turn)
    order = [place(lab, 1) for lab in range(devices)]
    rows = partial.shape[0]
    blocks = partial.reshape(rows, devices, width)
    blocks = jnp.where(turn == 1, blocks[:, order], blocks)
    bit = 1
    while bit < devices:
        count = blocks.shape[1]
        paired = blocks.reshape(rows, count // 2, 2, width)
        mine = mine_label & bit != 0
        keep = jnp.where(mine, paired[:, :, 1], paired[:, :, 0])
        send = jnp.where(mine, paired[:, :, 0], paired[:, :, 1])
        pairs = []
        for c in range(chains):
            for t in range(devices):
                partner = place(label(t, c % 2) ^ bit, c % 2)
                pairs.append((c * devices + t, c * devices + partner))
        blocks = keep + lax.ppermute(send, (rows_axis, axis), pairs)
        bit *= 2
    return blocks.reshape(rows, width)


def ssd_core(values, b_rows, c_rows, step_size, decay_rate, state):
    length, heads, head_dim = values.shape
    groups = b_rows.shape[1]
    per_group = heads // groups
    blocks = length // SPAN
    lower_mask = (jnp.arange(SPAN)[:, None] >= jnp.arange(SPAN)[None, :])[None]

    def blocked(array):
        return array.reshape((blocks, SPAN) + array.shape[1:])

    def ssd_advance(carry, item):
        value_blk, b_blk, c_blk, step_blk = item
        cums = jnp.cumsum(-step_blk * decay_rate[None, :], axis=0)
        diff = cums.T[:, :, None] - cums.T[:, None, :]
        weight = jnp.where(lower_mask, jnp.exp(jnp.where(lower_mask, diff, 0.0)), 0.0)
        scores = jnp.einsum("tgn,sgn->gts", c_blk, b_blk, precision=HIGH)
        scores = jnp.repeat(scores, per_group, axis=0)
        inputs = step_blk[:, :, None] * value_blk
        inside = jnp.einsum("hts,shp->thp", scores * weight, inputs, precision=HIGH)
        c_head = jnp.repeat(c_blk, per_group, axis=1)
        b_head = jnp.repeat(b_blk, per_group, axis=1)
        carried = jnp.exp(cums)[:, :, None] * jnp.einsum(
            "thn,hpn->thp", c_head, carry, precision=HIGH
        )
        tail = jnp.exp(cums[-1][None, :] - cums)
        fresh = jnp.einsum("shp,shn->hpn", tail[:, :, None] * inputs, b_head, precision=HIGH)
        carry = jnp.exp(cums[-1])[:, None, None] * carry + fresh
        return (carry, inside + carried)

    final, outputs = lax.scan(
        jax.checkpoint(ssd_advance),
        state,
        (blocked(values), blocked(b_rows), blocked(c_rows), blocked(step_size)),
    )
    return (outputs.reshape(length, heads, head_dim), final)


def local_states(values, b_rows, step_size, decay_rate):
    length, heads, head_dim = values.shape
    groups = b_rows.shape[1]
    per_group = heads // groups
    blocks = length // SPAN

    def blocked(array):
        return array.reshape((blocks, SPAN) + array.shape[1:])

    def local_advance(carry, item):
        value_blk, b_blk, step_blk = item
        cums = jnp.cumsum(-step_blk * decay_rate[None, :], axis=0)
        tail = jnp.exp(cums[-1][None, :] - cums)
        b_head = jnp.repeat(b_blk, per_group, axis=1)
        inputs = (tail * step_blk)[:, :, None] * value_blk
        fresh = jnp.einsum("shp,shn->hpn", inputs, b_head, precision=HIGH)
        return (jnp.exp(cums[-1])[:, None, None] * carry + fresh, None)

    start = jnp.zeros((heads, head_dim, STATE), jnp.float32)
    final, unused = lax.scan(
        local_advance, start, (blocked(values), blocked(b_rows), blocked(step_size))
    )
    return final


def local_adjoint(d_mixed, c_rows, step_size, decay_rate):
    length, heads, head_dim = d_mixed.shape
    groups = c_rows.shape[1]
    per_group = heads // groups
    blocks = length // SPAN

    def blocked(array):
        return array.reshape((blocks, SPAN) + array.shape[1:])

    def retreat(carry, item):
        grad_blk, c_blk, step_blk = item
        cums = jnp.cumsum(-step_blk * decay_rate[None, :], axis=0)
        c_head = jnp.repeat(c_blk, per_group, axis=1)
        weighted = jnp.exp(cums)[:, :, None] * grad_blk
        term = jnp.einsum("thp,thn->hpn", weighted, c_head, precision=HIGH)
        return (term + jnp.exp(cums[-1])[:, None, None] * carry, None)

    start = jnp.zeros((heads, head_dim, STATE), jnp.float32)
    final, unused = lax.scan(
        retreat, start, (blocked(d_mixed), blocked(c_rows), blocked(step_size)), reverse=True
    )
    return final


def doubled_rows(x, axis, order):
    devices, position = (lax.axis_size(axis), lax.axis_index(axis))
    for b in order:
        bit = 1 << b
        other = lax.ppermute(x, axis, [(i, i ^ bit) for i in range(devices)])
        low = position & bit == 0
        x = jnp.where(low, jnp.concatenate([x, other], 0), jnp.concatenate([other, x], 0))
    rows = x.shape[0] // devices
    x = x.reshape((2,) * len(order) + (rows,) + x.shape[1:])
    axes = [len(order) - 1 - order.index(b) for b in reversed(range(len(order)))]
    x = jnp.transpose(x, axes + list(range(len(order), x.ndim)))
    return x.reshape((devices * rows,) + x.shape[len(order) + 1 :])


def row_block(w, index, size):
    return lax.dynamic_slice_in_dim(w, index * size, size, axis=0)


def per_device(tokens, w_in, w_bc, w_dt, dt_bias, decay_rate, skip_gain, w_out, cotangent):
    devices = lax.axis_size("tp")
    rows, width = tokens.shape
    heads = decay_rate.shape[0]
    inner = w_in.shape[1]
    pair_cols = w_bc.shape[1]
    groups = pair_cols // (2 * STATE)
    out_cols = w_out.shape[0]
    w_all = lax.all_gather(
        jnp.concatenate([w_out.T, w_in, w_bc, w_dt], axis=1), "ctx", axis=0, tiled=True
    )
    bits = devices.bit_length() - 1
    pieces = doubled_rows(
        jnp.concatenate([tokens, cotangent], axis=1), "tp", list(reversed(range(bits)))
    )
    projected = None
    d_flat = None
    for k in range(devices):
        block = w_all[k * width : (k + 1) * width]
        piece = pieces[k * rows : (k + 1) * rows]
        term = jnp.dot(piece[:, :width], block[:, out_cols:], preferred_element_type=jnp.float32)
        projected = term if projected is None else projected + term
        term = jnp.dot(piece[:, width:], block[:, :out_cols], preferred_element_type=jnp.float32)
        d_flat = term if d_flat is None else d_flat + term
    values = projected[:, :inner].astype(jnp.bfloat16)
    pairs = projected[:, inner : inner + pair_cols].astype(jnp.bfloat16)
    pre_step = projected[:, inner + pair_cols :] + dt_bias[None, :]
    step_size = jax.nn.softplus(pre_step)
    value_f = values.astype(jnp.float32).reshape(rows, heads, HEADDIM)
    paired = pairs.astype(jnp.float32).reshape(rows, groups, 2, STATE)
    b_rows = paired[:, :, 0]
    c_rows = paired[:, :, 1]
    end_state = local_states(value_f, b_rows, step_size, decay_rate)
    decay_total = jnp.exp(-jnp.sum(step_size * decay_rate[None, :], axis=0))
    d_mixed = d_flat.reshape(rows, heads, HEADDIM)
    own_adjoint = local_adjoint(d_mixed, c_rows, step_size, decay_rate)
    state_in, adjoint = both_carries(decay_total, end_state, own_adjoint, "ctx")

    def with_state(vals, brows, crows, steps):
        return ssd_core(vals, brows, crows, steps, decay_rate, state_in)

    (core_out, core_end), pullback = jax.vjp(with_state, value_f, b_rows, c_rows, step_size)
    mixed = (
        (core_out + skip_gain[None, :, None] * value_f).reshape(rows, inner).astype(jnp.bfloat16)
    )
    partial_out = lax.dot_general(
        mixed, w_all[:, :out_cols], (((1,), (1,)), ((), ())), preferred_element_type=jnp.float32
    )
    output = scattered_sum(partial_out, "ctx", "tp", width).astype(jnp.bfloat16)
    grads = pullback((d_mixed, adjoint))
    d_values = grads[0] + skip_gain[None, :, None] * d_mixed
    d_pre = grads[3] * jax.nn.sigmoid(pre_step)
    d_pairs = jnp.stack([grads[1], grads[2]], axis=2).reshape(rows, pair_cols)
    d_cat = jnp.concatenate(
        [
            d_values.reshape(rows, inner).astype(jnp.bfloat16),
            d_pairs.astype(jnp.bfloat16),
            d_pre.astype(jnp.bfloat16),
        ],
        axis=1,
    )
    partial_grad = lax.dot_general(
        d_cat, w_all[:, out_cols:], (((1,), (1,)), ((), ())), preferred_element_type=jnp.float32
    )
    grad = scattered_sum(partial_grad, "ctx", "tp", width).astype(jnp.bfloat16)
    return (output, grad)


def solution(mesh):
    placed = (
        P("ctx", "tp"),
        P("ctx", "tp"),
        P("ctx", "tp"),
        P("ctx", "tp"),
        P("tp"),
        P("tp"),
        P("tp"),
        P("tp", "ctx"),
        P("ctx", "tp"),
    )
    return jax.shard_map(
        per_device,
        mesh=mesh,
        in_specs=placed,
        out_specs=(P("ctx", "tp"), P("ctx", "tp")),
        check_vma=False,
    )
```

profile of v0, /device:TPU:9, one launch (start us, length us, event | category | flops | bytes accessed | tf_op | source)
XLA Modules:
  0.0 366.3 jit_solution(14436932147277387907)
XLA Ops:
  8.0 1.4 pad_maximum_fusion.6
  11.3 6.6 %collective-permute-start = (bf16[256,512]{1,0:T(8,128)(2,1)S(1)}, bf16[256,512]{1,0:T(8,128)(2,1)S(1)}, u32[]{:S(2)}, u32[]{:S(2)}) collective-permute-start(bf16[256,512]{1,0:T(8,128)(2,1)S(1)} %constant_dynamic-update-slice_fusion), channel_id=1, source_target_pairs={{0,4},{1,5},{2,6},{3,7},{4,0},{5,1},{6,2},{7,3},{8,12},{9,13},{10,... | collective-permute-start | bytes 786440 | tf_op jit(solution)/shard_map/ppermute | solution.py:184
  17.8 9.1 %collective-permute-done = bf16[256,512]{1,0:T(8,128)(2,1)S(1)} collective-permute-done((bf16[256,512]{1,0:T(8,128)(2,1)S(1)}, bf16[256,512]{1,0:T(8,128)(2,1)S(1)}, u32[]{:S(2)}, u32[]{:S(2)}) %collective-permute-start) | collective-permute-done | bytes 262176 | tf_op jit(solution)/shard_map/ppermute | solution.py:184
  27.1 4.7 %collective-permute-start.1 = (bf16[512,512]{1,0:T(8,128)(2,1)S(1)}, bf16[512,512]{1,0:T(8,128)(2,1)S(1)}, u32[]{:S(2)}, u32[]{:S(2)}) collective-permute-start(bf16[512,512]{1,0:T(8,128)(2,1)S(1)} %maximum_select_fusion.2), channel_id=1, source_target_pairs={{0,2},{1,3},{2,0},{3,1},{4,6},{5,7},{6,4},{7,5},{8,10},{9,11},{10,... | collective-permute-start | bytes 1572872 | tf_op jit(solution)/shard_map/ppermute | solution.py:184
  31.8 8.0 %collective-permute-done.1 = bf16[512,512]{1,0:T(8,128)(2,1)S(1)} collective-permute-done((bf16[512,512]{1,0:T(8,128)(2,1)S(1)}, bf16[512,512]{1,0:T(8,128)(2,1)S(1)}, u32[]{:S(2)}, u32[]{:S(2)}) %collective-permute-start.1) | collective-permute-done | bytes 524320 | tf_op jit(solution)/shard_map/ppermute | solution.py:184
  40.3 3.1 collective-permute-start.2
  43.4 18.3 %collective-permute-done.2 = bf16[1024,512]{1,0:T(8,128)(2,1)S(1)} collective-permute-done((bf16[1024,512]{1,0:T(8,128)(2,1)S(1)}, bf16[1024,512]{1,0:T(8,128)(2,1)S(1)}, u32[]{:S(2)}, u32[]{:S(2)}) %collective-permute-start.2) | collective-permute-done | bytes 1048608 | tf_op jit(solution)/shard_map/ppermute | solution.py:184
  62.5 75.4 %all-gather.2.cloned.1.call-done = bf16[2048,1288]{1,0:T(8,128)(2,1)} async-done(((bf16[32,1288]{1,0:T(8,128)(2,1)}), bf16[2048,1288]{1,0:T(8,128)(2,1)}) %all-gather.2.cloned.1.call-update) | async-done | bytes 5275664 | tf_op jit(solution)/shard_map/all_gather | solution.py:206
  139.3 1.5 convolution_add_fusion.6
  140.7 1.7 convolution_add_fusion.5
  142.4 1.3 convolution_add_fusion.4
  144.4 1.3 convolution_add_fusion.1
  151.0 1.4 fusion.86
  163.3 2.2 collective-permute-start.3
  165.5 1.8 collective-permute-done.3
  168.6 4.3 %collective-permute-start.4 = (f32[8,8320]{1,0:T(8,128)}, f32[8,8320]{1,0:T(8,128)S(1)}, u32[]{:S(2)}, u32[]{:S(2)}) collective-permute-start(f32[8,8320]{1,0:T(8,128)} %pad_maximum_fusion.1), channel_id=1, source_target_pairs={{0,16},{8,24},{16,0},{24,8},{32,48},{40,56},{48,32},{56,40},{64,80... | collective-permute-start | bytes 798728 | tf_op jit(solution)/shard_map/ppermute | solution.py:45
  172.9 6.7 %collective-permute-done.4 = f32[8,8320]{1,0:T(8,128)S(1)} collective-permute-done((f32[8,8320]{1,0:T(8,128)}, f32[8,8320]{1,0:T(8,128)S(1)}, u32[]{:S(2)}, u32[]{:S(2)}) %collective-permute-start.4) | collective-permute-done | bytes 266272 | tf_op jit(solution)/shard_map/ppermute | solution.py:45
  180.7 4.3 %collective-permute-start.5 = (f32[8,8320]{1,0:T(8,128)}, f32[8,8320]{1,0:T(8,128)}, u32[]{:S(2)}, u32[]{:S(2)}) collective-permute-start(f32[8,8320]{1,0:T(8,128)} %pad_maximum_fusion.2), channel_id=1, source_target_pairs={{0,32},{8,40},{16,48},{24,56},{32,0},{40,8},{48,16},{56,24},{64,96... | collective-permute-start | bytes 798728 | tf_op jit(solution)/shard_map/ppermute | solution.py:45
  184.9 12.0 %collective-permute-done.5 = f32[8,8320]{1,0:T(8,128)} collective-permute-done((f32[8,8320]{1,0:T(8,128)}, f32[8,8320]{1,0:T(8,128)}, u32[]{:S(2)}, u32[]{:S(2)}) %collective-permute-start.5) | collective-permute-done | bytes 266272 | tf_op jit(solution)/shard_map/ppermute | solution.py:45
  199.5 6.3 %collective-permute-start.6 = (f32[8,8320]{1,0:T(8,128)}, f32[8,8320]{1,0:T(8,128)}, u32[]{:S(2)}, u32[]{:S(2)}) collective-permute-start(f32[8,8320]{1,0:T(8,128)} %pad_maximum_fusion.3), channel_id=1, source_target_pairs={{0,64},{8,72},{16,80},{24,88},{32,96},{40,104},{48,112},{56,120},{... | collective-permute-start | bytes 798728 | tf_op jit(solution)/shard_map/ppermute | solution.py:45
  206.5 11.8 %collective-permute-done.6 = f32[8,8320]{1,0:T(8,128)} collective-permute-done((f32[8,8320]{1,0:T(8,128)}, f32[8,8320]{1,0:T(8,128)}, u32[]{:S(2)}, u32[]{:S(2)}) %collective-permute-start.6) | collective-permute-done | bytes 266272 | tf_op jit(solution)/shard_map/ppermute | solution.py:45
  220.9 1.9 collective-permute-start.7
  224.4 4.7 %collective-permute-done.7 = f32[8,8320]{1,0:T(8,128)} collective-permute-done((f32[8,8320]{1,0:T(8,128)}, f32[8,8320]{1,0:T(8,128)}, u32[]{:S(2)}, u32[]{:S(2)}) %collective-permute-start.7) | collective-permute-done | bytes 266272 | tf_op jit(solution)/shard_map/ppermute | solution.py:45
  232.3 6.8 %collective-permute-done.8 = f32[8,8192]{1,0:T(8,128)S(1)} collective-permute-done((f32[8,8192]{1,0:T(8,128)S(1)}, f32[8,8192]{1,0:T(8,128)S(1)}, u32[]{:S(2)}, u32[]{:S(2)}) %collective-permute-start.8) | collective-permute-done | bytes 262176 | tf_op jit(solution)/shard_map/ppermute | solution.py:40
  240.4 6.8 %collective-permute-start.9 = (f32[8,8192]{1,0:T(8,128)S(1)}, f32[8,8192]{1,0:T(8,128)S(1)}, u32[]{:S(2)}, u32[]{:S(2)}) collective-permute-start(f32[8,8192]{1,0:T(8,128)S(1)} %add_select_fusion), channel_id=1, source_target_pairs={{0,8},{8,0},{16,24},{24,16},{32,40},{40,32},{48,56},{56,48},{64,72... | collective-permute-start | bytes 786440 | tf_op jit(solution)/shard_map/ppermute | solution.py:54
  247.3 2.2 fusion.12
  251.1 1.7 fusion.20
  256.0 2.2 fusion.22
  258.3 1.9 multiply_reduce_fusion.1
  261.1 2.5 reduce-window.44
  265.4 3.3 fusion
  268.7 2.8 reshape.520
  271.5 1.6 copy.209
  274.6 3.7 %gather_fusion.1 = f32[8,256,256]{2,1,0:T(8,128)} fusion(f32[256,8,256]{2,0,1:T(8,128)} %bitcast.319, s32[1024]{0:T(1024)} %pad_clamp_fusion), kind=kCustom, calls=%fused_computation.1 | custom fusion | bytes 4194336 | tf_op jit(solution)/shard_map/gather | solution.py:76
  278.3 2.1 gather_fusion
  280.5 2.0 bitcast_select_fusion
  283.7 3.7 collective-permute-start.10
  289.2 3.2 collective-permute-start.13
  292.4 8.5 %collective-permute-done.10 = f32[256,4,256]{2,0,1:T(8,128)} collective-permute-done((f32[256,4,256]{2,0,1:T(8,128)}, f32[256,4,256]{2,0,1:T(8,128)}, u32[]{:S(2)}, u32[]{:S(2)}) %collective-permute-start.10) | collective-permute-done | bytes 1048608 | tf_op jit(solution)/shard_map/ppermute | solution.py:89
  300.9 2.1 bitcast_add_fusion.1
  303.1 2.3 collective-permute-start.11
  305.4 9.8 %collective-permute-done.13 = f32[256,4,256]{2,0,1:T(8,128)} collective-permute-done((f32[256,4,256]{2,0,1:T(8,128)}, f32[256,4,256]{2,0,1:T(8,128)}, u32[]{:S(2)}, u32[]{:S(2)}) %collective-permute-start.13) | collective-permute-done | bytes 1048608 | tf_op jit(solution)/shard_map/ppermute | solution.py:89
  315.3 1.4 bitcast_add_fusion
  318.6 2.2 collective-permute-start.14
  320.9 12.9 %collective-permute-start.12 = (f32[256,1,256]{2,0,1:T(8,128)S(1)}, f32[256,1,256]{2,0,1:T(8,128)S(1)}, u32[]{:S(2)}, u32[]{:S(2)}) collective-permute-start(f32[256,1,256]{2,0,1:T(8,128)S(1)} %select_bitcast_fusion.6), channel_id=1, source_target_pairs={{0,4},{1,5},{2,6},{3,7},{4,0},{5,1},{6,2},{7,3},{8,12},{9,13},{10,... | collective-permute-start | bytes 786440 | tf_op jit(solution)/shard_map/ppermute | solution.py:89
  333.9 1.9 collective-permute-done.14
  336.9 7.8 %collective-permute-start.15 = (f32[256,1,256]{2,0,1:T(8,128)S(1)}, f32[256,1,256]{2,0,1:T(8,128)S(1)}, u32[]{:S(2)}, u32[]{:S(2)}) collective-permute-start(f32[256,1,256]{2,0,1:T(8,128)S(1)} %select_bitcast_fusion.4), channel_id=1, source_target_pairs={{0,4},{1,5},{2,6},{3,7},{4,0},{5,1},{6,2},{7,3},{8,12},{9,13},{10,... | collective-permute-start | bytes 786440 | tf_op jit(solution)/shard_map/ppermute | solution.py:89
  345.4 13.3 %collective-permute-done.15 = f32[256,1,256]{2,0,1:T(8,128)S(1)} collective-permute-done((f32[256,1,256]{2,0,1:T(8,128)S(1)}, f32[256,1,256]{2,0,1:T(8,128)S(1)}, u32[]{:S(2)}, u32[]{:S(2)}) %collective-permute-start.15) | collective-permute-done | bytes 262176 | tf_op jit(solution)/shard_map/ppermute | solution.py:89
  (194 shorter events, 52.7 us)
Async XLA Ops:
  7.2 130.8 %all-gather.2.cloned.1.call-start = ((), (), s32[]{:S(2)}) async-start(), calls=%async_computation | async-start | bytes 5857280 | tf_op jit(solution)/shard_map/all_gather | solution.py:206
  11.3 15.6 %collective-permute-start = (bf16[256,512]{1,0:T(8,128)(2,1)S(1)}, bf16[256,512]{1,0:T(8,128)(2,1)S(1)}, u32[]{:S(2)}, u32[]{:S(2)}) collective-permute-start(bf16[256,512]{1,0:T(8,128)(2,1)S(1)} %constant_dynamic-update-slice_fusion), channel_id=1, source_target_pairs={{0,4},{1,5},{2,6},{3,7},{4,0},{5,1},{6,2},{7,3},{8,12},{9,13},{10,... | collective-permute-start | bytes 786440 | tf_op jit(solution)/shard_map/ppermute | solution.py:184
  27.1 12.7 %collective-permute-start.1 = (bf16[512,512]{1,0:T(8,128)(2,1)S(1)}, bf16[512,512]{1,0:T(8,128)(2,1)S(1)}, u32[]{:S(2)}, u32[]{:S(2)}) collective-permute-start(bf16[512,512]{1,0:T(8,128)(2,1)S(1)} %maximum_select_fusion.2), channel_id=1, source_target_pairs={{0,2},{1,3},{2,0},{3,1},{4,6},{5,7},{6,4},{7,5},{8,10},{9,11},{10,... | collective-permute-start | bytes 1572872 | tf_op jit(solution)/shard_map/ppermute | solution.py:184
  40.3 21.5 %collective-permute-start.2 = (bf16[1024,512]{1,0:T(8,128)(2,1)S(1)}, bf16[1024,512]{1,0:T(8,128)(2,1)S(1)}, u32[]{:S(2)}, u32[]{:S(2)}) collective-permute-start(bf16[1024,512]{1,0:T(8,128)(2,1)S(1)} %maximum_select_fusion.1), channel_id=1, source_target_pairs={{0,1},{1,0},{2,3},{3,2},{4,5},{5,4},{6,7},{7,6},{8,9},{9,8},{10,11... | collective-permute-start | bytes 3145736 | tf_op jit(solution)/shard_map/ppermute | solution.py:184
  62.5 81.6 %copy-start.6 = (bf16[2,2,2,256,512]{4,3,2,1,0:T(8,128)(2,1)}, bf16[2,2,2,256,512]{4,3,2,1,0:T(8,128)(2,1)S(1)}, u32[]{:S(2)}) copy-start(bf16[2,2,2,256,512]{4,3,2,1,0:T(8,128)(2,1)S(1)} %copy.125) | copy-start | bytes 6291460
  139.2 4.5 %copy-start.1 = (bf16[2048,1288]{1,0:T(8,128)(2,1)S(1)}, bf16[2048,1288]{1,0:T(8,128)(2,1)}, u32[]{:S(2)}) copy-start(bf16[2048,1288]{1,0:T(8,128)(2,1)} %all-gather.2.cloned.1.call-done) | copy-start | bytes 15826948
  144.4 3.6 copy-start.23
  144.4 3.6 copy-start.28
  144.4 14.5 %slice-start = ((s8[5767168]{0:T(1024)(128)(4,1)}), s8[1572864]{0:T(1024)(128)(4,1)S(1)}, s32[]{:S(2)}) async-start(s8[5767168]{0:T(1024)(128)(4,1)} %bitcast.294), calls=%async_computation.1 | async-start | bytes 3145728
  148.2 5.6 %copy-start.26 = (f32[8]{0:T(128)}, f32[8]{0:T(128)S(1)}, u32[]{:S(2)}) copy-start(f32[8]{0:T(128)S(1)} %get-tuple-element.201) | copy-start | bytes 100
  148.8 1.0 copy-start.16
  149.1 12.3 %copy-start.18 = (f32[256,8]{0,1:T(8,128)}, f32[256,8]{0,1:T(8,128)S(1)}, u32[]{:S(2)}) copy-start(f32[256,8]{0,1:T(8,128)S(1)} %get-tuple-element.199) | copy-start | bytes 24580
  150.8 10.5 %copy-start.13 = (f32[256,128]{1,0:T(8,128)}, f32[256,128]{1,0:T(8,128)S(1)}, u32[]{:S(2)}) copy-start(f32[256,128]{1,0:T(8,128)S(1)} %copy.136) | copy-start | bytes 393220
  151.0 8.0 %slice-start.1 = ((s8[5767168]{0:T(1024)(128)(4,1)}), s8[4194304]{0:T(1024)(128)(4,1)S(1)}, s32[]{:S(2)}) async-start(s8[5767168]{0:T(1024)(128)(4,1)} %bitcast.294), calls=%async_computation.2 | async-start | bytes 8388608
  161.3 6.1 %copy-start.27 = (f32[8]{0:T(128)S(1)}, f32[8]{0:T(128)}, u32[]{:S(2)}) copy-start(f32[8]{0:T(128)} %copy-done.26) | copy-start | bytes 100
  163.3 4.0 %collective-permute-start.3 = (f32[8,16512]{1,0:T(8,128)}, f32[8,16512]{1,0:T(8,128)S(1)}, u32[]{:S(2)}, u32[]{:S(2)}) collective-permute-start(f32[8,16512]{1,0:T(8,128)} %pad_maximum_fusion), channel_id=1, source_target_pairs={{0,8},{8,0},{16,24},{24,16},{32,40},{40,32},{48,56},{56,48},{64,72... | collective-permute-start | bytes 1585160 | tf_op jit(solution)/shard_map/ppermute | solution.py:21
  168.6 54.3 %copy-start.30 = (s32[8]{0:T(128)S(1)}, s32[8]{0:T(128)}, u32[]{:S(2)}) copy-start(s32[8]{0:T(128)} %constant.154) | copy-start | bytes 100
  168.6 11.1 %collective-permute-start.4 = (f32[8,8320]{1,0:T(8,128)}, f32[8,8320]{1,0:T(8,128)S(1)}, u32[]{:S(2)}, u32[]{:S(2)}) collective-permute-start(f32[8,8320]{1,0:T(8,128)} %pad_maximum_fusion.1), channel_id=1, source_target_pairs={{0,16},{8,24},{16,0},{24,8},{32,48},{40,56},{48,32},{56,40},{64,80... | collective-permute-start | bytes 798728 | tf_op jit(solution)/shard_map/ppermute | solution.py:45
  179.8 43.7 %copy-start.29 = (f32[8]{0:T(128)S(1)}, f32[8]{0:T(128)}, u32[]{:S(2)}) copy-start(f32[8]{0:T(128)} %param.17) | copy-start | bytes 100
  179.8 44.5 %copy-start.12 = (bf16[256,256]{0,1:T(8,128)(2,1)S(1)}, bf16[256,256]{0,1:T(8,128)(2,1)}, u32[]{:S(2)}) copy-start(bf16[256,256]{0,1:T(8,128)(2,1)} %copy-done.11) | copy-start | bytes 393220
  180.7 16.2 %collective-permute-start.5 = (f32[8,8320]{1,0:T(8,128)}, f32[8,8320]{1,0:T(8,128)}, u32[]{:S(2)}, u32[]{:S(2)}) collective-permute-start(f32[8,8320]{1,0:T(8,128)} %pad_maximum_fusion.2), channel_id=1, source_target_pairs={{0,32},{8,40},{16,48},{24,56},{32,0},{40,8},{48,16},{56,24},{64,96... | collective-permute-start | bytes 798728 | tf_op jit(solution)/shard_map/ppermute | solution.py:45
  199.5 18.8 %collective-permute-start.6 = (f32[8,8320]{1,0:T(8,128)}, f32[8,8320]{1,0:T(8,128)}, u32[]{:S(2)}, u32[]{:S(2)}) collective-permute-start(f32[8,8320]{1,0:T(8,128)} %pad_maximum_fusion.3), channel_id=1, source_target_pairs={{0,64},{8,72},{16,80},{24,88},{32,96},{40,104},{48,112},{56,120},{... | collective-permute-start | bytes 798728 | tf_op jit(solution)/shard_map/ppermute | solution.py:45
  219.1 28.1 %copy-start.17 = (f32[8,2,128]{2,0,1:T(8,128)S(1)}, f32[8,2,128]{2,0,1:T(8,128)}, u32[]{:S(2)}) copy-start(f32[8,2,128]{2,0,1:T(8,128)} %copy-done.16) | copy-start | bytes 24580
  219.1 28.2 %copy-start.22 = (f32[8,2]{0,1:T(2,128)S(1)}, f32[8,2]{0,1:T(2,128)}, u32[]{:S(2)}) copy-start(f32[8,2]{0,1:T(2,128)} %copy-done.21) | copy-start | bytes 196
  220.9 8.2 %collective-permute-start.7 = (f32[8,8320]{1,0:T(8,128)}, f32[8,8320]{1,0:T(8,128)}, u32[]{:S(2)}, u32[]{:S(2)}) collective-permute-start(f32[8,8320]{1,0:T(8,128)} %pad_maximum_fusion.4), channel_id=1, source_target_pairs={{0,128},{8,136},{16,144},{24,152},{32,160},{40,168},{48,176},{56,1... | collective-permute-start | bytes 798728 | tf_op jit(solution)/shard_map/ppermute | solution.py:45
  230.9 8.1 %collective-permute-start.8 = (f32[8,8192]{1,0:T(8,128)S(1)}, f32[8,8192]{1,0:T(8,128)S(1)}, u32[]{:S(2)}, u32[]{:S(2)}) collective-permute-start(f32[8,8192]{1,0:T(8,128)S(1)} %add_select_fusion.4), channel_id=1, source_target_pairs={{0,256},{16,272},{32,288},{48,304},{64,320},{80,336},{96,352},{112... | collective-permute-start | bytes 786440 | tf_op jit(solution)/shard_map/ppermute | solution.py:40
  240.4 9.2 %collective-permute-start.9 = (f32[8,8192]{1,0:T(8,128)S(1)}, f32[8,8192]{1,0:T(8,128)S(1)}, u32[]{:S(2)}, u32[]{:S(2)}) collective-permute-start(f32[8,8192]{1,0:T(8,128)S(1)} %add_select_fusion), channel_id=1, source_target_pairs={{0,8},{8,0},{16,24},{24,16},{32,40},{40,32},{48,56},{56,48},{64,72... | collective-permute-start | bytes 786440 | tf_op jit(solution)/shard_map/ppermute | solution.py:54
  247.3 2.6 copy-start.24
  247.3 3.8 %copy-start.14 = (f32[256,128]{1,0:T(8,128)S(1)}, f32[256,128]{1,0:T(8,128)}, u32[]{:S(2)}) copy-start(f32[256,128]{1,0:T(8,128)} %copy-done.13) | copy-start | bytes 393220
  247.3 3.8 %copy-start.19 = (f32[256,8]{0,1:T(8,128)S(1)}, f32[256,8]{0,1:T(8,128)}, u32[]{:S(2)}) copy-start(f32[256,8]{0,1:T(8,128)} %copy-done.18) | copy-start | bytes 24580
  249.6 3.8 %copy-start.9 = (f32[256,1,128]{0,2,1:T(8,128)S(1)}, f32[256,1,128]{0,2,1:T(8,128)}, u32[]{:S(2)}) copy-start(f32[256,1,128]{0,2,1:T(8,128)} %get-tuple-element.186) | copy-start | bytes 393220
  250.7 3.8 %copy-start.10 = (f32[256,1,128]{0,2,1:T(8,128)S(1)}, f32[256,1,128]{0,2,1:T(8,128)}, u32[]{:S(2)}) copy-start(f32[256,1,128]{0,2,1:T(8,128)} %get-tuple-element.184) | copy-start | bytes 393220
  253.4 2.6 copy-start.20
  258.3 5.4 %copy-start.25 = (f32[8]{0:T(128)S(1)}, f32[8]{0:T(128)}, u32[]{:S(2)}) copy-start(f32[8]{0:T(128)} %param.16) | copy-start | bytes 100
  271.5 2.3 slice-start.2
  280.5 6.9 %copy-start.8 = (f32[8,256,256]{2,1,0:T(8,128)S(1)}, f32[8,256,256]{2,1,0:T(8,128)}, u32[]{:S(2)}) copy-start(f32[8,256,256]{2,1,0:T(8,128)} %gather_fusion.1) | copy-start | bytes 6291460
  282.5 5.6 %copy-start = (f32[256,8,256]{2,0,1:T(8,128)}, f32[256,8,256]{2,0,1:T(8,128)S(1)}, u32[]{:S(2)}) copy-start(f32[256,8,256]{2,0,1:T(8,128)S(1)} %bitcast_select_fusion) | copy-start | bytes 6291460
  282.5 4.9 %copy-start.7 = (f32[256,4,2,256]{3,2,1,0:T(2,128)S(1)}, f32[256,4,2,256]{3,2,1,0:T(2,128)}, u32[]{:S(2)}) copy-start(f32[256,4,2,256]{3,2,1,0:T(2,128)} %reshape.520) | copy-start | bytes 6291460
  283.7 17.2 %collective-permute-start.10 = (f32[256,4,256]{2,0,1:T(8,128)}, f32[256,4,256]{2,0,1:T(8,128)}, u32[]{:S(2)}, u32[]{:S(2)}) collective-permute-start(f32[256,4,256]{2,0,1:T(8,128)} %select_bitcast_fusion.1), channel_id=1, source_target_pairs={{0,1},{1,0},{2,3},{3,2},{4,5},{5,4},{6,7},{7,6},{8,11},{9,10},{10,... | collective-permute-start | bytes 3145736 | tf_op jit(solution)/shard_map/ppermute | solution.py:89
  289.2 26.0 %collective-permute-start.13 = (f32[256,4,256]{2,0,1:T(8,128)}, f32[256,4,256]{2,0,1:T(8,128)}, u32[]{:S(2)}, u32[]{:S(2)}) collective-permute-start(f32[256,4,256]{2,0,1:T(8,128)} %select_bitcast_fusion), channel_id=1, source_target_pairs={{0,1},{1,0},{2,3},{3,2},{4,5},{5,4},{6,7},{7,6},{8,11},{9,10},{10,... | collective-permute-start | bytes 3145736 | tf_op jit(solution)/shard_map/ppermute | solution.py:89
  303.0 2.4 copy-start.4
  303.1 17.7 %collective-permute-start.11 = (f32[256,2,256]{2,0,1:T(8,128)S(1)}, f32[256,2,256]{2,0,1:T(8,128)S(1)}, u32[]{:S(2)}, u32[]{:S(2)}) collective-permute-start(f32[256,2,256]{2,0,1:T(8,128)S(1)} %select_bitcast_fusion.3), channel_id=1, source_target_pairs={{0,2},{1,3},{2,0},{3,1},{4,6},{5,7},{6,4},{7,5},{8,10},{9,11},{10,... | collective-permute-start | bytes 1572872 | tf_op jit(solution)/shard_map/ppermute | solution.py:89
  316.7 1.0 copy-start.2
  316.7 4.1 %copy-start.5 = (f32[256,4,256]{2,0,1:T(8,128)S(1)}, f32[256,4,256]{2,0,1:T(8,128)}, u32[]{:S(2)}) copy-start(f32[256,4,256]{2,0,1:T(8,128)} %copy-done.4) | copy-start | bytes 3145732
  318.6 17.2 %copy-start.3 = (f32[256,4,256]{2,0,1:T(8,128)S(1)}, f32[256,4,256]{2,0,1:T(8,128)}, u32[]{:S(2)}) copy-start(f32[256,4,256]{2,0,1:T(8,128)} %copy-done.2) | copy-start | bytes 3145732
  318.6 17.1 %collective-permute-start.14 = (f32[256,2,256]{2,0,1:T(8,128)}, f32[256,2,256]{2,0,1:T(8,128)}, u32[]{:S(2)}, u32[]{:S(2)}) collective-permute-start(f32[256,2,256]{2,0,1:T(8,128)} %select_bitcast_fusion.2), channel_id=1, source_target_pairs={{0,2},{1,3},{2,0},{3,1},{4,6},{5,7},{6,4},{7,5},{8,10},{9,11},{10,... | collective-permute-start | bytes 1572872 | tf_op jit(solution)/shard_map/ppermute | solution.py:89
  320.9 23.8 %collective-permute-start.12 = (f32[256,1,256]{2,0,1:T(8,128)S(1)}, f32[256,1,256]{2,0,1:T(8,128)S(1)}, u32[]{:S(2)}, u32[]{:S(2)}) collective-permute-start(f32[256,1,256]{2,0,1:T(8,128)S(1)} %select_bitcast_fusion.6), channel_id=1, source_target_pairs={{0,4},{1,5},{2,6},{3,7},{4,0},{5,1},{6,2},{7,3},{8,12},{9,13},{10,... | collective-permute-start | bytes 786440 | tf_op jit(solution)/shard_map/ppermute | solution.py:89
  336.9 21.8 %collective-permute-start.15 = (f32[256,1,256]{2,0,1:T(8,128)S(1)}, f32[256,1,256]{2,0,1:T(8,128)S(1)}, u32[]{:S(2)}, u32[]{:S(2)}) collective-permute-start(f32[256,1,256]{2,0,1:T(8,128)S(1)} %select_bitcast_fusion.4), channel_id=1, source_target_pairs={{0,4},{1,5},{2,6},{3,7},{4,0},{5,1},{6,2},{7,3},{8,12},{9,13},{10,... | collective-permute-start | bytes 786440 | tf_op jit(solution)/shard_map/ppermute | solution.py:89
  (3 other events, 2.5 us)
Sparse Core Ops, SparseCore 0:
  10.7 127.1 all-gather.1
where the time goes:
time: 368 us; the launch traced here: 366 us
  waiting for transfers between devices  188 us (51%)
  starting transfers between devices  73.5 us (20%)
  matrix products  35.3 us (10%)
  other arithmetic  32.3 us (9%)
  local copies, waits for them, and re-layouts  22.1 us (6%)
  between operations  15 us (4%)
    all_gather x1, waiting for transfers between devices, per_device(): lax.all_gather(jnp.concatenate([w_out.T, w_in, w_bc, w_dt], axis=1), 'ctx...  75.4 us
    ppermute x3, waiting for transfers between devices, doubled_rows(): other = lax.ppermute(x, axis, [(i, i ^ bit) for i in range(devices)])  35.4 us
    ppermute x4, waiting for transfers between devices, both_carries(): got = lax.ppermute(message, axis, [(i, i ^ bit) for i in range(devices)])  35.2 us
    ppermute x6, waiting for transfers between devices, scattered_sum(): blocks = keep + lax.ppermute(send, (rows_axis, axis), pairs)  33.5 us
    ppermute x6, starting transfers between devices, scattered_sum(): blocks = keep + lax.ppermute(send, (rows_axis, axis), pairs)  32 us
    ppermute x4, starting transfers between devices, both_carries(): got = lax.ppermute(message, axis, [(i, i ^ bit) for i in range(devices)])  16.8 us
    ppermute x3, starting transfers between devices, doubled_rows(): other = lax.ppermute(x, axis, [(i, i ^ bit) for i in range(devices)])  14.3 us
    dot_general x8, matrix products, per_device(): jnp.dot(piece[:, width:], block[:, :out_cols], preferred_element_type=jnp...  10.3 us
  transfers between devices with their start and end apart: 17, of which 14 were waited for; matrix products, arithmetic and copies ran while one was open for 4% of the time, Pallas kernels for 0%

commit v1 on v0

--- a/solution.py
+++ b/solution.py
@@ -8,6 +8,13 @@
 SPAN = 256
 HIGH = lax.Precision.HIGH
 RING = 4
+
+
+def swapped_in(x, name, dim):
+    peers = lax.axis_size(name)
+    tiles = jnp.stack([x for _ in range(peers)])
+    tiles = lax.all_to_all(tiles, name, split_axis=0, concat_axis=0)
+    return jnp.concatenate(tiles, axis=dim)
 
 
 def both_carries(decay, forward, backward, axis):
@@ -203,9 +210,7 @@
     pair_cols = w_bc.shape[1]
     groups = pair_cols // (2 * STATE)
     out_cols = w_out.shape[0]
-    w_all = lax.all_gather(
-        jnp.concatenate([w_out.T, w_in, w_bc, w_dt], axis=1), "ctx", axis=0, tiled=True
-    )
+    w_all = swapped_in(jnp.concatenate([w_out.T, w_in, w_bc, w_dt], axis=1), "ctx", 0)
     bits = devices.bit_length() - 1
     pieces = doubled_rows(
         jnp.concatenate([tokens, cotangent], axis=1), "tp", list(reversed(range(bits)))

time: 368 us -> 438 us (1.19)
  the two profiles are of different devices: /device:TPU:9 before, /device:TPU:56 now
where the time goes in v1:
time: 438 us; the launch traced here: 437 us
  waiting for transfers between devices  243 us (55%)
  starting transfers between devices  87.4 us (20%)
  other arithmetic  36.8 us (8%)
  matrix products  34.5 us (8%)
  local copies, waits for them, and re-layouts  33.7 us (8%)
    ppermute x3, waiting for transfers between devices, doubled_rows(): other = lax.ppermute(x, axis, [(i, i ^ bit) for i in range(devices)])  161 us
    ppermute x4, waiting for transfers between devices, both_carries(): got = lax.ppermute(message, axis, [(i, i ^ bit) for i in range(devices)])  35 us
    ppermute x6, waiting for transfers between devices, scattered_sum(): blocks = keep + lax.ppermute(send, (rows_axis, axis), pairs)  34.8 us
    ppermute x4, starting transfers between devices, both_carries(): got = lax.ppermute(message, axis, [(i, i ^ bit) for i in range(devices)])  27.2 us
    ppermute x6, starting transfers between devices, scattered_sum(): blocks = keep + lax.ppermute(send, (rows_axis, axis), pairs)  27.2 us
    all_to_all x1, starting transfers between devices, swapped_in(): tiles = lax.all_to_all(tiles, name, split_axis=0, concat_axis=0)  14.6 us
    ppermute x3, starting transfers between devices, doubled_rows(): other = lax.ppermute(x, axis, [(i, i ^ bit) for i in range(devices)])  13 us
    ppermute x1, waiting for transfers between devices, both_carries(): got_m = lax.ppermute(total_m, axis, wanted)  10.2 us
  transfers between devices with their start and end apart: 17, of which 13 were waited for; matrix products, arithmetic and copies ran while one was open for 6% of the time, Pallas kernels for 0%

profile of v1, /device:TPU:56, one launch (start us, length us, event | category | flops | bytes accessed | tf_op | source)
XLA Modules:
  0.0 436.8 jit_solution(8335467657005837384)
XLA Ops:
  2.2 2.9 stack.5
  5.1 14.6 %all-to-all-start = ((bf16[64,32,1288]{2,1,0:T(8,128)(2,1)}), bf16[64,32,1288]{2,1,0:T(8,128)(2,1)}, u32[]{:S(2)}, u32[]{:S(2)}) async-start(bf16[64,32,1288]{2,1,0:T(8,128)(2,1)} %stack.5), calls=%async_computation | async-start | bytes 11534336 | tf_op jit(solution)/shard_map/all_to_all | solution.py:16
  19.8 4.7 %collective-permute-start = (bf16[256,512]{1,0:T(8,128)(2,1)S(1)}, bf16[256,512]{1,0:T(8,128)(2,1)S(1)}, u32[]{:S(2)}, u32[]{:S(2)}) collective-permute-start(bf16[256,512]{1,0:T(8,128)(2,1)S(1)} %constant_dynamic-update-slice_fusion), channel_id=1, source_target_pairs={{0,4},{1,5},{2,6},{3,7},{4,0},{5,1},{6,2},{7,3},{8,12},{9,13},{10,... | collective-permute-start | bytes 786440 | tf_op jit(solution)/shard_map/ppermute | solution.py:191
  24.6 126.5 %collective-permute-done = bf16[256,512]{1,0:T(8,128)(2,1)S(1)} collective-permute-done((bf16[256,512]{1,0:T(8,128)(2,1)S(1)}, bf16[256,512]{1,0:T(8,128)(2,1)S(1)}, u32[]{:S(2)}, u32[]{:S(2)}) %collective-permute-start) | collective-permute-done | bytes 262176 | tf_op jit(solution)/shard_map/ppermute | solution.py:191
  151.3 4.9 %collective-permute-start.1 = (bf16[512,512]{1,0:T(8,128)(2,1)S(1)}, bf16[512,512]{1,0:T(8,128)(2,1)S(1)}, u32[]{:S(2)}, u32[]{:S(2)}) collective-permute-start(bf16[512,512]{1,0:T(8,128)(2,1)S(1)} %maximum_select_fusion.2), channel_id=1, source_target_pairs={{0,2},{1,3},{2,0},{3,1},{4,6},{5,7},{6,4},{7,5},{8,10},{9,11},{10,... | collective-permute-start | bytes 1572872 | tf_op jit(solution)/shard_map/ppermute | solution.py:191
  156.3 11.9 %collective-permute-done.1 = bf16[512,512]{1,0:T(8,128)(2,1)S(1)} collective-permute-done((bf16[512,512]{1,0:T(8,128)(2,1)S(1)}, bf16[512,512]{1,0:T(8,128)(2,1)S(1)}, u32[]{:S(2)}, u32[]{:S(2)}) %collective-permute-start.1) | collective-permute-done | bytes 524320 | tf_op jit(solution)/shard_map/ppermute | solution.py:191
  168.6 3.4 collective-permute-start.2
  172.0 22.2 %collective-permute-done.2 = bf16[1024,512]{1,0:T(8,128)(2,1)S(1)} collective-permute-done((bf16[1024,512]{1,0:T(8,128)(2,1)S(1)}, bf16[1024,512]{1,0:T(8,128)(2,1)S(1)}, u32[]{:S(2)}, u32[]{:S(2)}) %collective-permute-start.2) | collective-permute-done | bytes 1048608 | tf_op jit(solution)/shard_map/ppermute | solution.py:191
  195.0 3.3 fusion.145
  208.0 1.7 copy.127
  223.5 1.9 collective-permute-start.3
  225.4 2.1 collective-permute-done.3
  228.8 5.5 %collective-permute-start.4 = (f32[8,8320]{1,0:T(8,128)}, f32[8,8320]{1,0:T(8,128)}, u32[]{:S(2)}, u32[]{:S(2)}) collective-permute-start(f32[8,8320]{1,0:T(8,128)} %pad_maximum_fusion.1), channel_id=1, source_target_pairs={{0,16},{8,24},{16,0},{24,8},{32,48},{40,56},{48,32},{56,40},{64,80... | collective-permute-start | bytes 798728 | tf_op jit(solution)/shard_map/ppermute | solution.py:52
  234.2 7.0 %collective-permute-done.4 = f32[8,8320]{1,0:T(8,128)} collective-permute-done((f32[8,8320]{1,0:T(8,128)}, f32[8,8320]{1,0:T(8,128)}, u32[]{:S(2)}, u32[]{:S(2)}) %collective-permute-start.4) | collective-permute-done | bytes 266272 | tf_op jit(solution)/shard_map/ppermute | solution.py:52
  243.9 8.2 %collective-permute-start.5 = (f32[8,8320]{1,0:T(8,128)}, f32[8,8320]{1,0:T(8,128)}, u32[]{:S(2)}, u32[]{:S(2)}) collective-permute-start(f32[8,8320]{1,0:T(8,128)} %pad_maximum_fusion.2), channel_id=1, source_target_pairs={{0,32},{8,40},{16,48},{24,56},{32,0},{40,8},{48,16},{56,24},{64,96... | collective-permute-start | bytes 798728 | tf_op jit(solution)/shard_map/ppermute | solution.py:52
  252.1 11.9 %collective-permute-done.5 = f32[8,8320]{1,0:T(8,128)} collective-permute-done((f32[8,8320]{1,0:T(8,128)}, f32[8,8320]{1,0:T(8,128)}, u32[]{:S(2)}, u32[]{:S(2)}) %collective-permute-start.5) | collective-permute-done | bytes 266272 | tf_op jit(solution)/shard_map/ppermute | solution.py:52
  266.6 11.7 %collective-permute-start.6 = (f32[8,8320]{1,0:T(8,128)}, f32[8,8320]{1,0:T(8,128)}, u32[]{:S(2)}, u32[]{:S(2)}) collective-permute-start(f32[8,8320]{1,0:T(8,128)} %pad_maximum_fusion.3), channel_id=1, source_target_pairs={{0,64},{8,72},{16,80},{24,88},{32,96},{40,104},{48,112},{56,120},{... | collective-permute-start | bytes 798728 | tf_op jit(solution)/shard_map/ppermute | solution.py:52
  279.0 11.0 %collective-permute-done.6 = f32[8,8320]{1,0:T(8,128)} collective-permute-done((f32[8,8320]{1,0:T(8,128)}, f32[8,8320]{1,0:T(8,128)}, u32[]{:S(2)}, u32[]{:S(2)}) %collective-permute-start.6) | collective-permute-done | bytes 266272 | tf_op jit(solution)/shard_map/ppermute | solution.py:52
  292.7 1.9 collective-permute-start.7
  296.1 5.2 %collective-permute-done.7 = f32[8,8320]{1,0:T(8,128)} collective-permute-done((f32[8,8320]{1,0:T(8,128)}, f32[8,8320]{1,0:T(8,128)}, u32[]{:S(2)}, u32[]{:S(2)}) %collective-permute-start.7) | collective-permute-done | bytes 266272 | tf_op jit(solution)/shard_map/ppermute | solution.py:52
  304.4 10.2 %collective-permute-done.8 = f32[8,8192]{1,0:T(8,128)S(1)} collective-permute-done((f32[8,8192]{1,0:T(8,128)S(1)}, f32[8,8192]{1,0:T(8,128)S(1)}, u32[]{:S(2)}, u32[]{:S(2)}) %collective-permute-start.8) | collective-permute-done | bytes 262176 | tf_op jit(solution)/shard_map/ppermute | solution.py:47
  314.6 1.4 add_select_fusion
  316.0 2.1 collective-permute-start.9
  318.2 3.2 slice.466
  321.4 2.3 fusion.12
  326.8 2.8 fusion.22
  332.1 3.6 multiply_reduce_fusion.1
  337.0 2.5 reduce-window.44
  339.6 1.4 fusion.20
  342.7 3.3 fusion
  346.1 2.8 reshape.534
  348.9 1.6 copy.209
  350.5 3.7 gather_fusion.1
  354.2 2.9 copy_select_fusion
  357.3 3.8 collective-permute-start.13
  361.0 2.1 fusion.90
  363.1 3.8 gather_fusion
  366.9 2.6 bitcast_select_fusion
  371.9 2.4 collective-permute-start.10
  374.3 1.6 bitcast_add_fusion
  376.0 4.9 %collective-permute-start.14 = (f32[256,2,256]{2,0,1:T(8,128)S(1)}, f32[256,2,256]{2,0,1:T(8,128)S(1)}, u32[]{:S(2)}, u32[]{:S(2)}) collective-permute-start(f32[256,2,256]{2,0,1:T(8,128)S(1)} %select_bitcast_fusion.2), channel_id=1, source_target_pairs={{0,2},{1,3},{2,0},{3,1},{4,6},{5,7},{6,4},{7,5},{8,10},{9,11},{10,... | collective-permute-start | bytes 1572872 | tf_op jit(solution)/shard_map/ppermute | solution.py:96
  380.9 13.5 %collective-permute-done.10 = f32[256,4,256]{2,0,1:T(8,128)} collective-permute-done((f32[256,4,256]{2,0,1:T(8,128)}, f32[256,4,256]{2,0,1:T(8,128)}, u32[]{:S(2)}, u32[]{:S(2)}) %collective-permute-start.10) | collective-permute-done | bytes 1048608 | tf_op jit(solution)/shard_map/ppermute | solution.py:96
  394.5 1.4 bitcast_add_fusion.1
  396.8 4.6 %collective-permute-start.11 = (f32[256,2,256]{2,0,1:T(8,128)}, f32[256,2,256]{2,0,1:T(8,128)}, u32[]{:S(2)}, u32[]{:S(2)}) collective-permute-start(f32[256,2,256]{2,0,1:T(8,128)} %select_bitcast_fusion.3), channel_id=1, source_target_pairs={{0,2},{1,3},{2,0},{3,1},{4,6},{5,7},{6,4},{7,5},{8,10},{9,11},{10,... | collective-permute-start | bytes 1572872 | tf_op jit(solution)/shard_map/ppermute | solution.py:96
  401.7 5.7 %collective-permute-start.15 = (f32[256,1,256]{2,0,1:T(8,128)S(1)}, f32[256,1,256]{2,0,1:T(8,128)S(1)}, u32[]{:S(2)}, u32[]{:S(2)}) collective-permute-start(f32[256,1,256]{2,0,1:T(8,128)S(1)} %select_bitcast_fusion.4), channel_id=1, source_target_pairs={{0,4},{1,5},{2,6},{3,7},{4,0},{5,1},{6,2},{7,3},{8,12},{9,13},{10,... | collective-permute-start | bytes 786440 | tf_op jit(solution)/shard_map/ppermute | solution.py:96
  407.4 7.8 %collective-permute-done.11 = f32[256,2,256]{2,0,1:T(8,128)} collective-permute-done((f32[256,2,256]{2,0,1:T(8,128)}, f32[256,2,256]{2,0,1:T(8,128)}, u32[]{:S(2)}, u32[]{:S(2)}) %collective-permute-start.11) | collective-permute-done | bytes 524320 | tf_op jit(solution)/shard_map/ppermute | solution.py:96
  416.4 5.7 %collective-permute-start.12 = (f32[256,1,256]{2,0,1:T(8,128)S(1)}, f32[256,1,256]{2,0,1:T(8,128)S(1)}, u32[]{:S(2)}, u32[]{:S(2)}) collective-permute-start(f32[256,1,256]{2,0,1:T(8,128)S(1)} %select_bitcast_fusion.6), channel_id=1, source_target_pairs={{0,4},{1,5},{2,6},{3,7},{4,0},{5,1},{6,2},{7,3},{8,12},{9,13},{10,... | collective-permute-start | bytes 786440 | tf_op jit(solution)/shard_map/ppermute | solution.py:96
  422.8 13.3 %collective-permute-done.12 = f32[256,1,256]{2,0,1:T(8,128)S(1)} collective-permute-done((f32[256,1,256]{2,0,1:T(8,128)S(1)}, f32[256,1,256]{2,0,1:T(8,128)S(1)}, u32[]{:S(2)}, u32[]{:S(2)}) %collective-permute-start.12) | collective-permute-done | bytes 262176 | tf_op jit(solution)/shard_map/ppermute | solution.py:96
  (211 shorter events, 55.8 us)
Async XLA Ops:
  5.1 14.7 %copy-start.26 = (bf16[256,256]{1,0:T(8,128)(2,1)S(1)}, bf16[256,256]{1,0:T(8,128)(2,1)}, u32[]{:S(2)}) copy-start(bf16[256,256]{1,0:T(8,128)(2,1)} %param.11) | copy-start | bytes 393220
  5.1 14.7 %copy-start.27 = (bf16[256,256]{1,0:T(8,128)(2,1)S(1)}, bf16[256,256]{1,0:T(8,128)(2,1)}, u32[]{:S(2)}) copy-start(bf16[256,256]{1,0:T(8,128)(2,1)} %param.19) | copy-start | bytes 393220
  5.1 189.8 %all-to-all-start = ((bf16[64,32,1288]{2,1,0:T(8,128)(2,1)}), bf16[64,32,1288]{2,1,0:T(8,128)(2,1)}, u32[]{:S(2)}, u32[]{:S(2)}) async-start(bf16[64,32,1288]{2,1,0:T(8,128)(2,1)} %stack.5), calls=%async_computation | async-start | bytes 11534336 | tf_op jit(solution)/shard_map/all_to_all | solution.py:16
  19.8 131.2 %collective-permute-start = (bf16[256,512]{1,0:T(8,128)(2,1)S(1)}, bf16[256,512]{1,0:T(8,128)(2,1)S(1)}, u32[]{:S(2)}, u32[]{:S(2)}) collective-permute-start(bf16[256,512]{1,0:T(8,128)(2,1)S(1)} %constant_dynamic-update-slice_fusion), channel_id=1, source_target_pairs={{0,4},{1,5},{2,6},{3,7},{4,0},{5,1},{6,2},{7,3},{8,12},{9,13},{10,... | collective-permute-start | bytes 786440 | tf_op jit(solution)/shard_map/ppermute | solution.py:191
  151.3 16.8 %collective-permute-start.1 = (bf16[512,512]{1,0:T(8,128)(2,1)S(1)}, bf16[512,512]{1,0:T(8,128)(2,1)S(1)}, u32[]{:S(2)}, u32[]{:S(2)}) collective-permute-start(bf16[512,512]{1,0:T(8,128)(2,1)S(1)} %maximum_select_fusion.2), channel_id=1, source_target_pairs={{0,2},{1,3},{2,0},{3,1},{4,6},{5,7},{6,4},{7,5},{8,10},{9,11},{10,... | collective-permute-start | bytes 1572872 | tf_op jit(solution)/shard_map/ppermute | solution.py:191
  168.6 25.6 %collective-permute-start.2 = (bf16[1024,512]{1,0:T(8,128)(2,1)S(1)}, bf16[1024,512]{1,0:T(8,128)(2,1)S(1)}, u32[]{:S(2)}, u32[]{:S(2)}) collective-permute-start(bf16[1024,512]{1,0:T(8,128)(2,1)S(1)} %maximum_select_fusion.1), channel_id=1, source_target_pairs={{0,1},{1,0},{2,3},{3,2},{4,5},{5,4},{6,7},{7,6},{8,9},{9,8},{10,11... | collective-permute-start | bytes 3145736 | tf_op jit(solution)/shard_map/ppermute | solution.py:191
  198.3 2.6 copy-start.10
  198.3 2.6 copy-start.3
  203.5 2.3 copy-start.24
  218.3 9.3 %copy-start.37 = (f32[8]{0:T(128)S(1)}, f32[8]{0:T(128)}, u32[]{:S(2)}) copy-start(f32[8]{0:T(128)} %get-tuple-element.201) | copy-start | bytes 100
  223.5 4.0 collective-permute-start.3
  228.8 65.8 %copy-start.41 = (s32[8]{0:T(128)S(1)}, s32[8]{0:T(128)}, u32[]{:S(2)}) copy-start(s32[8]{0:T(128)} %constant.154) | copy-start | bytes 100
  228.8 12.5 %collective-permute-start.4 = (f32[8,8320]{1,0:T(8,128)}, f32[8,8320]{1,0:T(8,128)}, u32[]{:S(2)}, u32[]{:S(2)}) collective-permute-start(f32[8,8320]{1,0:T(8,128)} %pad_maximum_fusion.1), channel_id=1, source_target_pairs={{0,16},{8,24},{16,0},{24,8},{32,48},{40,56},{48,32},{56,40},{64,80... | collective-permute-start | bytes 798728 | tf_op jit(solution)/shard_map/ppermute | solution.py:52
  242.0 53.2 %copy-start.40 = (f32[8]{0:T(128)S(1)}, f32[8]{0:T(128)}, u32[]{:S(2)}) copy-start(f32[8]{0:T(128)} %param.17) | copy-start | bytes 100
  242.0 53.9 %copy-start.14 = (bf16[256,256]{0,1:T(8,128)(2,1)S(1)}, bf16[256,256]{0,1:T(8,128)(2,1)}, u32[]{:S(2)}) copy-start(bf16[256,256]{0,1:T(8,128)(2,1)} %copy-done.13) | copy-start | bytes 393220
  243.9 20.1 %collective-permute-start.5 = (f32[8,8320]{1,0:T(8,128)}, f32[8,8320]{1,0:T(8,128)}, u32[]{:S(2)}, u32[]{:S(2)}) collective-permute-start(f32[8,8320]{1,0:T(8,128)} %pad_maximum_fusion.2), channel_id=1, source_target_pairs={{0,32},{8,40},{16,48},{24,56},{32,0},{40,8},{48,16},{56,24},{64,96... | collective-permute-start | bytes 798728 | tf_op jit(solution)/shard_map/ppermute | solution.py:52
  266.6 23.4 %collective-permute-start.6 = (f32[8,8320]{1,0:T(8,128)}, f32[8,8320]{1,0:T(8,128)}, u32[]{:S(2)}, u32[]{:S(2)}) collective-permute-start(f32[8,8320]{1,0:T(8,128)} %pad_maximum_fusion.3), channel_id=1, source_target_pairs={{0,64},{8,72},{16,80},{24,88},{32,96},{40,104},{48,112},{56,120},{... | collective-permute-start | bytes 798728 | tf_op jit(solution)/shard_map/ppermute | solution.py:52
  290.8 27.4 %copy-start.25 = (f32[8,2,128]{2,0,1:T(8,128)S(1)}, f32[8,2,128]{2,0,1:T(8,128)}, u32[]{:S(2)}) copy-start(f32[8,2,128]{2,0,1:T(8,128)} %copy-done.24) | copy-start | bytes 24580
  292.7 8.6 %collective-permute-start.7 = (f32[8,8320]{1,0:T(8,128)}, f32[8,8320]{1,0:T(8,128)}, u32[]{:S(2)}, u32[]{:S(2)}) collective-permute-start(f32[8,8320]{1,0:T(8,128)} %pad_maximum_fusion.4), channel_id=1, source_target_pairs={{0,128},{8,136},{16,144},{24,152},{32,160},{40,168},{48,176},{56,1... | collective-permute-start | bytes 798728 | tf_op jit(solution)/shard_map/ppermute | solution.py:52
  303.1 11.5 %collective-permute-start.8 = (f32[8,8192]{1,0:T(8,128)S(1)}, f32[8,8192]{1,0:T(8,128)S(1)}, u32[]{:S(2)}, u32[]{:S(2)}) collective-permute-start(f32[8,8192]{1,0:T(8,128)S(1)} %add_select_fusion.4), channel_id=1, source_target_pairs={{0,256},{16,272},{32,288},{48,304},{64,320},{80,336},{96,352},{112... | collective-permute-start | bytes 786440 | tf_op jit(solution)/shard_map/ppermute | solution.py:47
  316.0 7.7 %collective-permute-start.9 = (f32[8,8192]{1,0:T(8,128)S(1)}, f32[8,8192]{1,0:T(8,128)S(1)}, u32[]{:S(2)}, u32[]{:S(2)}) collective-permute-start(f32[8,8192]{1,0:T(8,128)S(1)} %add_select_fusion), channel_id=1, source_target_pairs={{0,8},{8,0},{16,24},{24,16},{32,40},{40,32},{48,56},{56,48},{64,72... | collective-permute-start | bytes 786440 | tf_op jit(solution)/shard_map/ppermute | solution.py:61
  318.2 3.2 copy-start.28
  321.4 2.7 copy-start.30
  323.7 2.3 copy-start.11
  323.7 2.3 copy-start.12
  325.0 4.5 %copy-start.22 = (f32[256,8]{0,1:T(8,128)}, f32[256,8]{0,1:T(8,128)S(1)}, u32[]{:S(2)}) copy-start(f32[256,8]{0,1:T(8,128)S(1)} %get-tuple-element.196) | copy-start | bytes 24580
  325.5 4.0 copy-start.31
  326.3 3.2 copy-start.19
  332.1 3.7 copy-start.23
  332.1 3.7 copy-start.32
  332.1 4.8 %copy-start.33 = (f32[8,256]{1,0:T(8,128)S(1)}, f32[8,256]{1,0:T(8,128)}, u32[]{:S(2)}) copy-start(f32[8,256]{1,0:T(8,128)} %get-tuple-element.190) | copy-start | bytes 24580
  332.1 4.8 %copy-start.34 = (f32[8,256]{1,0:T(8,128)S(1)}, f32[8,256]{1,0:T(8,128)}, u32[]{:S(2)}) copy-start(f32[8,256]{1,0:T(8,128)} %get-tuple-element.191) | copy-start | bytes 24580
  332.1 7.5 %copy-start.17 = (f32[256,8,64]{0,2,1:T(8,128)S(1)}, f32[256,8,64]{0,2,1:T(8,128)}, u32[]{:S(2)}) copy-start(f32[256,8,64]{0,2,1:T(8,128)} %fusion.12) | copy-start | bytes 1572868
  335.8 5.2 %copy-start.20 = (bf16[256,1,1,128]{0,3,2,1:T(8,128)(2,1)S(1)}, bf16[256,1,1,128]{0,3,2,1:T(8,128)(2,1)}, u32[]{:S(2)}) copy-start(bf16[256,1,1,128]{0,3,2,1:T(8,128)(2,1)} %fusion.32) | copy-start | bytes 196612
  335.8 5.2 %copy-start.21 = (bf16[256,1,1,128]{0,3,2,1:T(8,128)(2,1)S(1)}, bf16[256,1,1,128]{0,3,2,1:T(8,128)(2,1)}, u32[]{:S(2)}) copy-start(bf16[256,1,1,128]{0,3,2,1:T(8,128)(2,1)} %fusion.31) | copy-start | bytes 196612
  335.8 5.3 %copy-start.35 = (f32[256,8]{0,1:T(8,128)S(1)}, f32[256,8]{0,1:T(8,128)}, u32[]{:S(2)}) copy-start(f32[256,8]{0,1:T(8,128)} %get-tuple-element.194) | copy-start | bytes 24580
  335.8 5.3 %copy-start.39 = (f32[8]{0:T(128)S(1)}, f32[8]{0:T(128)}, u32[]{:S(2)}) copy-start(f32[8]{0:T(128)} %param.15) | copy-start | bytes 100
  335.8 6.1 %copy-start.18 = (f32[256,8,64]{0,2,1:T(8,128)S(1)}, f32[256,8,64]{0,2,1:T(8,128)}, u32[]{:S(2)}) copy-start(f32[256,8,64]{0,2,1:T(8,128)} %get-tuple-element.213) | copy-start | bytes 1572868
  335.8 6.1 %copy-start.36 = (f32[512]{0:T(512)S(1)}, f32[512]{0:T(512)}, u32[]{:S(2)}) copy-start(f32[512]{0:T(512)} %mul.540) | copy-start | bytes 6148
  357.1 3.9 copy-start.2
  357.1 3.9 copy-start.15
  357.3 17.1 %collective-permute-start.13 = (f32[256,4,256]{2,0,1:T(8,128)S(1)}, f32[256,4,256]{2,0,1:T(8,128)}, u32[]{:S(2)}, u32[]{:S(2)}) collective-permute-start(f32[256,4,256]{2,0,1:T(8,128)S(1)} %select_bitcast_fusion), channel_id=1, source_target_pairs={{0,1},{1,0},{2,3},{3,2},{4,5},{5,4},{6,7},{7,6},{8,11},{9,10},{10,... | collective-permute-start | bytes 3145736 | tf_op jit(solution)/shard_map/ppermute | solution.py:96
  371.9 22.6 %collective-permute-start.10 = (f32[256,4,256]{2,0,1:T(8,128)}, f32[256,4,256]{2,0,1:T(8,128)}, u32[]{:S(2)}, u32[]{:S(2)}) collective-permute-start(f32[256,4,256]{2,0,1:T(8,128)} %select_bitcast_fusion.1), channel_id=1, source_target_pairs={{0,1},{1,0},{2,3},{3,2},{4,5},{5,4},{6,7},{7,6},{8,11},{9,10},{10,... | collective-permute-start | bytes 3145736 | tf_op jit(solution)/shard_map/ppermute | solution.py:96
  374.3 20.2 %copy-start.1 = (f32[256,8,256]{2,0,1:T(8,128)S(1)}, f32[256,8,256]{2,0,1:T(8,128)}, u32[]{:S(2)}) copy-start(f32[256,8,256]{2,0,1:T(8,128)} %copy-done) | copy-start | bytes 6291460
  376.0 25.6 %collective-permute-start.14 = (f32[256,2,256]{2,0,1:T(8,128)S(1)}, f32[256,2,256]{2,0,1:T(8,128)S(1)}, u32[]{:S(2)}, u32[]{:S(2)}) collective-permute-start(f32[256,2,256]{2,0,1:T(8,128)S(1)} %select_bitcast_fusion.2), channel_id=1, source_target_pairs={{0,2},{1,3},{2,0},{3,1},{4,6},{5,7},{6,4},{7,5},{8,10},{9,11},{10,... | collective-permute-start | bytes 1572872 | tf_op jit(solution)/shard_map/ppermute | solution.py:96
  396.8 18.4 %collective-permute-start.11 = (f32[256,2,256]{2,0,1:T(8,128)}, f32[256,2,256]{2,0,1:T(8,128)}, u32[]{:S(2)}, u32[]{:S(2)}) collective-permute-start(f32[256,2,256]{2,0,1:T(8,128)} %select_bitcast_fusion.3), channel_id=1, source_target_pairs={{0,2},{1,3},{2,0},{3,1},{4,6},{5,7},{6,4},{7,5},{8,10},{9,11},{10,... | collective-permute-start | bytes 1572872 | tf_op jit(solution)/shard_map/ppermute | solution.py:96
  401.7 20.4 %collective-permute-start.15 = (f32[256,1,256]{2,0,1:T(8,128)S(1)}, f32[256,1,256]{2,0,1:T(8,128)S(1)}, u32[]{:S(2)}, u32[]{:S(2)}) collective-permute-start(f32[256,1,256]{2,0,1:T(8,128)S(1)} %select_bitcast_fusion.4), channel_id=1, source_target_pairs={{0,4},{1,5},{2,6},{3,7},{4,0},{5,1},{6,2},{7,3},{8,12},{9,13},{10,... | collective-permute-start | bytes 786440 | tf_op jit(solution)/shard_map/ppermute | solution.py:96
  416.4 19.7 %collective-permute-start.12 = (f32[256,1,256]{2,0,1:T(8,128)S(1)}, f32[256,1,256]{2,0,1:T(8,128)S(1)}, u32[]{:S(2)}, u32[]{:S(2)}) collective-permute-start(f32[256,1,256]{2,0,1:T(8,128)S(1)} %select_bitcast_fusion.6), channel_id=1, source_target_pairs={{0,4},{1,5},{2,6},{3,7},{4,0},{5,1},{6,2},{7,3},{8,12},{9,13},{10,... | collective-permute-start | bytes 786440 | tf_op jit(solution)/shard_map/ppermute | solution.py:96
  (11 other events, 15.9 us)
